TPU v7x, 32 devices: a whole 2x2x4 slice. The times are simulated.
32 devices in a mesh: row: 4 (over x, core), col: 8 (over z, y).
Axes of the slice: x: 2, y: 2, z: 4, core: 2. Of those that a mesh axis runs over, the one named last changes fastest.
Arguments:
- amplitudes: float32 [8, 64, 512, 512], P(None, None, None, ('row', 'col')), may hold values from -6 to 6
- cycle_integrals: float32 [64, 512, 4, 512], P('col'), may hold values from -0.125 to 0.125
- occ_irrep: int32 [64], replicated, may hold values from 0 to 7
- virt_irrep: int32 [512], replicated, may hold values from 0 to 7
Outputs:
- cycle: float32 [8, 512, 2048], P(None, 'row', 'col')
All inputs are finite; a program needn't handle non-finite values.
Results may differ from a plain program's by a relative error of at most 0.0003.
Values sent between devices are 32-bit elements; how exact they have to be, the bound alone decides.
No kernel may reach another device: no remote copies, remote signals or barrier semaphores. Data moves between devices by JAX's collectives and lax.ppermute only.
A program may use at most 256 MiB of HBM per device.

v0:
```python
import jax
import jax.numpy as jnp
from jax import lax
from jax.sharding import PartitionSpec as P


def scatter_sum(flat, col_count, col_place):
    rows, a_local, width = flat.shape
    shard = width // col_count
    pairs_n = col_count // 2
    side = col_place % 2
    line = col_place // 2
    parts = flat.reshape(rows, a_local, pairs_n, 2, shard)
    keep = jnp.where(side == 0, parts[:, :, :, 0], parts[:, :, :, 1])
    give = jnp.where(side == 0, parts[:, :, :, 1], parts[:, :, :, 0])
    swap = [(q, q ^ 1) for q in range(col_count)]
    line_sum = keep + lax.ppermute(give, "col", swap)
    total = lax.dynamic_index_in_dim(line_sum, line, axis=2, keepdims=False)
    up_prev = None
    down_prev = None
    for t in range(pairs_n - 1):
        up_send = line_sum[:, :, t + 1 :]
        down_send = line_sum[:, :, : pairs_n - 1 - t]
        if up_prev is not None:
            up_send = up_send + up_prev[:, :, 1:]
            down_send = down_send + down_prev[:, :, :-1]
        payload = jnp.where(line == t, up_send, down_send)
        links = []
        for v in range(2):
            links.append((2 * t + v, 2 * (t + 1) + v))
            links.append((2 * (pairs_n - 1 - t) + v, 2 * (pairs_n - 2 - t) + v))
        got = lax.ppermute(payload, "col", links)
        up_prev = jnp.where(line == t + 1, got, 0.0)
        down_prev = jnp.where(line == pairs_n - 2 - t, got, 0.0)
        total = total + up_prev[:, :, 0] + down_prev[:, :, -1]
    return total


def per_device(amplitudes, cycle_integrals, occ_irrep, virt_irrep):
    slab_rows, occ_count, virt_count, c_local = amplitudes.shape
    col_count = lax.axis_size("col")
    row_count = lax.axis_size("row")
    k_local = occ_count // col_count
    a_local = virt_count // row_count
    column_slab = cycle_integrals.shape[2]
    col_place = lax.axis_index("col")
    row_place = lax.axis_index("row")
    k_irrep = lax.dynamic_slice_in_dim(occ_irrep, col_place * k_local, k_local)
    c_irrep = lax.dynamic_slice_in_dim(
        virt_irrep, (row_place * col_count + col_place) * c_local, c_local
    )
    slab_irrep = occ_irrep[:slab_rows]
    column_irrep = occ_irrep[:column_slab]
    int_sym = (
        k_irrep[:, None, None, None]
        ^ virt_irrep[None, :, None, None]
        ^ (column_irrep[None, None, :, None] ^ virt_irrep[None, None, None, :])
    )
    masked_ints = jnp.where(int_sym == 0, cycle_integrals, 0.0).reshape(
        k_local * virt_count, column_slab * virt_count
    )
    chunks = 2 if slab_rows % 2 == 0 else 1
    rows = slab_rows // chunks
    results = []
    for step in range(chunks):
        amps = amplitudes[step * rows : (step + 1) * rows]
        amp_sym = (
            slab_irrep[step * rows : (step + 1) * rows, None, None, None]
            ^ occ_irrep[None, :, None, None]
            ^ (virt_irrep[None, None, :, None] ^ c_irrep[None, None, None, :])
        )
        masked_amps = jnp.where(amp_sym == 0, amps, 0.0)
        grouped = masked_amps.reshape(rows, col_count, k_local, row_count, a_local, c_local)
        grouped = jnp.transpose(grouped, (0, 3, 1, 2, 4, 5)).reshape(
            rows, row_count * col_count, k_local, a_local, c_local
        )
        if step == 1 and chunks > 2:
            grouped, masked_ints = lax.optimization_barrier((grouped, masked_ints))
        if step >= 2:
            grouped, results[step - 2] = lax.optimization_barrier((grouped, results[step - 2]))
        items = lax.all_to_all(grouped, ("row", "col"), split_axis=1, concat_axis=4, tiled=True)
        blocks = jnp.transpose(items.reshape(rows, k_local, a_local, virt_count), (0, 2, 1, 3))
        blocks = blocks.reshape(rows, a_local, k_local * virt_count)
        partial_value = jnp.einsum(
            "iap,pq->iaq",
            blocks,
            masked_ints,
            precision=lax.Precision.HIGH,
            preferred_element_type=jnp.float32,
        )
        flat = partial_value.reshape(rows, a_local, column_slab * virt_count)
        results.append(lax.psum_scatter(flat, "col", scatter_dimension=2, tiled=True))
    return jnp.concatenate(results, axis=0)


def solution(mesh):
    placed = (P(None, None, None, ("row", "col")), P("col", None, None, None), P(), P())
    return jax.shard_map(
        per_device, mesh=mesh, in_specs=placed, out_specs=P(None, "row", "col"), check_vma=False
    )
```

profile of v0, /device:TPU:0, one launch (start us, length us, event | category | flops | bytes accessed | tf_op | source)
XLA Modules:
  0.0 593.7 jit_solution(1753503171140539836)
XLA Ops:
  6.5 0.8 fusion.1
  7.3 0.8 dynamic_slice.6
  8.1 0.8 broadcast_xor_fusion
  8.8 0.7 broadcast_xor_fusion.4
  9.6 11.0 %slice_select_fusion.1 = (f32[4,64,512,16]{2,3,1,0:T(8,128)}, f32[4,64,512,16]{2,3,1,0:T(8,128)}) fusion(f32[8,64,512,16]{2,3,1,0:T(8,128)} %param.4, s32[512,16]{0,1:T(8,128)S(1)} %broadcast_xor_fusion, s32[4,64]{1,0:T(4,128)S(1)} %get-tuple-element.7, s32[4,64]{1,0:T(4,128)S(1)} %get-tuple-element.8), kind=kLoop, calls=%fused_computation.4 | loop fusion | flops 12582912 | bytes 33589248 | tf_op jit(solution)/shard_map/jit(_where)/select_n | solution.py:72
  20.6 9.9 %reshape.185 = f32[4,8,8,4,128,16]{4,3,5,2,1,0:T(4,128)} reshape(f32[4,64,512,16]{2,3,1,0:T(8,128)} %get-tuple-element.5) | data formatting | bytes 16777216 | tf_op jit(solution)/shard_map/reshape | solution.py:73
  30.5 7.8 %copy.23 = f32[4,4,8,8,128,16]{4,5,3,0,2,1:T(8,128)} copy(f32[4,4,8,8,128,16]{4,1,5,3,2,0:T(4,128)} %bitcast.38) | data formatting | bytes 16777216 | tf_op jit(solution)/shard_map/reshape | solution.py:74
  38.3 7.4 %all-to-all-start = ((f32[4,32,8,128,16]{3,4,2,0,1:T(8,128)}), f32[4,32,8,128,16]{3,4,2,0,1:T(8,128)}, u32[]{:S(2)}, u32[]{:S(2)}) async-start(f32[4,32,8,128,16]{3,4,2,0,1:T(8,128)} %bitcast.37), calls=%async_computation | async-start | bytes 16777216 | tf_op jit(solution)/shard_map/all_to_all | solution.py:81
  45.7 9.9 %reshape.190 = f32[4,8,8,4,128,16]{4,3,5,2,1,0:T(4,128)} reshape(f32[4,64,512,16]{2,3,1,0:T(8,128)} %get-tuple-element.6) | data formatting | bytes 16777216 | tf_op jit(solution)/shard_map/reshape | solution.py:73
  55.7 7.9 %copy.25 = f32[4,4,8,8,128,16]{4,5,3,0,2,1:T(8,128)} copy(f32[4,4,8,8,128,16]{4,1,5,3,2,0:T(4,128)} %bitcast.39) | data formatting | bytes 16777216 | tf_op jit(solution)/shard_map/reshape | solution.py:74
  63.5 171.8 %all-to-all-done = f32[4,32,8,128,16]{3,4,2,0,1:T(8,128)} async-done(((f32[4,32,8,128,16]{3,4,2,0,1:T(8,128)}), f32[4,32,8,128,16]{3,4,2,0,1:T(8,128)}, u32[]{:S(2)}, u32[]{:S(2)}) %all-to-all-start) | async-done | bytes 8388640 | tf_op jit(solution)/shard_map/all_to_all | solution.py:81
  235.3 0.0 copy-start.1
  235.3 3.8 all-to-all-start.1
  239.1 0.2 reduce-scatter.3.cloned.1.call-start
  239.3 0.0 copy-done.1
  239.3 0.1 dynamic_slice.7
  239.4 0.0 copy-done
  239.4 0.1 broadcast_xor_fusion.2
  239.5 0.1 broadcast_xor_fusion.1
  239.6 23.1 %fusion = f32[8,512,4,512]{3,2,1,0:T(4,128)} fusion(f32[8,512,4,512]{3,2,1,0:T(4,128)} %param.5, s32[4,512]{1,0:T(4,128)S(1)} %broadcast_xor_fusion.2, s32[8,512]{1,0:T(8,128)S(1)} %broadcast_xor_fusion.1), kind=kLoop, calls=%fused_computation.1 | loop fusion | flops 25165824 | bytes 67133440 | tf_op jit(solution)/shard_map/jit(_where)/select_n | solution.py:59
  262.7 39.8 %reshape.194 = f32[4096,2048,1]{1,0,2:T(8,128)} reshape(f32[8,512,4,512]{3,2,1,0:T(4,128)} %fusion) | data formatting | bytes 67108864 | tf_op jit(solution)/shard_map/reshape | solution.py:59
  302.4 4.5 copy.17
  307.0 32.7 %fusion.2 = f32[4,128,2048]{2,1,0:T(8,128)} fusion(f32[4,128,4096]{1,2,0:T(8,128)S(1)} %bitcast.41, f32[4096,2048,1]{1,0,2:T(8,128)} %reshape.194), kind=kOutput, calls=%fused_computation.13 | convolution fusion | flops 25769803776 | bytes 46137344 | tf_op jit(solution)/shard_map/iap,pq->iaq/dot_general | solution.py:84
  339.7 0.0 reduce-scatter.3.cloned.1.call-update
  339.8 0.3 reduce-scatter.5.cloned.1.call-start
  340.0 122.3 %all-to-all-done.1 = f32[4,32,8,128,16]{3,4,2,0,1:T(8,128)} async-done(((f32[4,32,8,128,16]{3,4,2,0,1:T(8,128)}), f32[4,32,8,128,16]{3,4,2,0,1:T(8,128)}, u32[]{:S(2)}, u32[]{:S(2)}) %all-to-all-start.1) | async-done | bytes 8388640 | tf_op jit(solution)/shard_map/all_to_all | solution.py:81
  462.3 4.5 copy.21
  466.9 33.0 %fusion.3 = f32[4,128,2048]{2,1,0:T(8,128)} fusion(f32[4,128,4096]{1,2,0:T(8,128)S(1)} %bitcast.40, f32[4096,2048,1]{1,0,2:T(8,128)} %reshape.194), kind=kOutput, calls=%fused_computation.14 | convolution fusion | flops 25769803776 | bytes 46137344 | tf_op jit(solution)/shard_map/iap,pq->iaq/dot_general | solution.py:84
  499.9 0.0 reduce-scatter.5.cloned.1.call-update
  499.9 0.0 reduce-scatter.3.cloned.1.call-done
  499.9 84.6 %reduce-scatter.5.cloned.1.call-done = f32[4,128,256]{2,1,0:T(8,128)} async-done(((f32[4,128,2048]{2,1,0:T(8,128)}), f32[4,128,256]{2,1,0:T(8,128)}) %reduce-scatter.5.cloned.1.call-update) | async-done | bytes 524304 | tf_op jit(solution)/shard_map/reduce_scatter | solution.py:92
  584.6 2.2 pad_maximum_fusion
  (1 shorter events, 0.0 us)
Async XLA Ops:
  38.3 197.0 %all-to-all-start = ((f32[4,32,8,128,16]{3,4,2,0,1:T(8,128)}), f32[4,32,8,128,16]{3,4,2,0,1:T(8,128)}, u32[]{:S(2)}, u32[]{:S(2)}) async-start(f32[4,32,8,128,16]{3,4,2,0,1:T(8,128)} %bitcast.37), calls=%async_computation | async-start | bytes 16777216 | tf_op jit(solution)/shard_map/all_to_all | solution.py:81
  235.3 4.1 copy-start.1
  235.3 4.1 copy-start
  235.3 227.0 %all-to-all-start.1 = ((f32[4,32,8,128,16]{3,4,2,0,1:T(8,128)}), f32[4,32,8,128,16]{3,4,2,0,1:T(8,128)}, u32[]{:S(2)}, u32[]{:S(2)}) async-start(f32[4,32,8,128,16]{3,4,2,0,1:T(8,128)} %bitcast.36), calls=%async_computation.2 | async-start | bytes 16777216 | tf_op jit(solution)/shard_map/all_to_all | solution.py:81
  239.1 260.8 %reduce-scatter.3.cloned.1.call-start = ((), (), s32[]{:S(2)}) async-start(), calls=%async_computation.4 | async-start | bytes 4718592 | tf_op jit(solution)/shard_map/reduce_scatter | solution.py:92
  339.8 244.8 %reduce-scatter.5.cloned.1.call-start = ((), (), s32[]{:S(2)}) async-start(), calls=%async_computation.5 | async-start | bytes 4718592 | tf_op jit(solution)/shard_map/reduce_scatter | solution.py:92
Sparse Core Ops, SparseCore 0:
  339.9 149.7 reduce-scatter.2
  500.0 84.4 reduce-scatter.4
where the time goes:
time: 596 us; the launch traced here: 594 us
  waiting for transfers between devices  379 us (64%)
  local copies, waits for them, and re-layouts  86 us (14%)
  matrix products  65.8 us (11%)
  other arithmetic  38 us (6%)
  between operations  13.5 us (2%)
  starting transfers between devices  11.7 us (2%)
    all_to_all x2, waiting for transfers between devices, per_device(): lax.all_to_all(grouped, ('row', 'col'), split_axis=1, concat_axis=4, tile...  294 us
    reduce_scatter x2, waiting for transfers between devices, per_device(): lax.psum_scatter(flat, 'col', scatter_dimension=2, tiled=True)  84.6 us
    dot_general x2, matrix products, per_device(): jnp.einsum('iap,pq->iaq', blocks, masked_ints, precision=lax.Precision.HI...  65.8 us
    reshape x1, local copies, waits for them, and re-layouts, per_device(): jnp.where(int_sym == 0, cycle_integrals, 0.0)  39.8 us
    select_n x1, other arithmetic, per_device(): jnp.where(int_sym == 0, cycle_integrals, 0.0)  23.1 us
    reshape x2, local copies, waits for them, and re-layouts, per_device(): masked_amps.reshape(rows, col_count, k_local, row_count, a_local, c_local)  19.8 us
    reshape x2, local copies, waits for them, and re-layouts, per_device(): jnp.transpose(grouped, (0, 3, 1, 2, 4, 5))  15.6 us
  transfers between devices with their start and end apart: 4, of which 3 were waited for; matrix products, arithmetic and copies ran while one was open for 26% of the time, Pallas kernels for 0%

commit v1 on v0

--- a/solution.py
+++ b/solution.py
@@ -1,7 +1,21 @@
+import functools
 import jax
 import jax.numpy as jnp
 from jax import lax
 from jax.sharding import PartitionSpec as P
+
+
+def see_teams(field_in, net_axis):
+    taken_in = jnp.concatenate(
+        lax.all_to_all(
+            jnp.stack(jnp.split(field_in, lax.axis_size(net_axis), axis=1)), net_axis, 0, 0
+        ),
+        axis=4,
+    )
+    return taken_in
+
+
+write_the_wall = functools.partial(see_teams, net_axis=("row", "col"))
 
 
 def scatter_sum(flat, col_count, col_place):
@@ -78,7 +92,7 @@
             grouped, masked_ints = lax.optimization_barrier((grouped, masked_ints))
         if step >= 2:
             grouped, results[step - 2] = lax.optimization_barrier((grouped, results[step - 2]))
-        items = lax.all_to_all(grouped, ("row", "col"), split_axis=1, concat_axis=4, tiled=True)
+        items = write_the_wall(grouped)
         blocks = jnp.transpose(items.reshape(rows, k_local, a_local, virt_count), (0, 2, 1, 3))
         blocks = blocks.reshape(rows, a_local, k_local * virt_count)
         partial_value = jnp.einsum(

time: 596 us -> 622 us (1.044)
  local copies, waits for them, and re-layouts: 86 us -> 139 us
  waiting for transfers between devices: 379 us -> 353 us
    unnamed x4 -> x70, local copies, waits for them, and re-layouts: 0.01 us -> 47 us
    all_to_all x2, waiting for transfers between devices: 294 us -> 268 us  [see_teams(): lax.all_to_all(jnp.stack(jnp.split(field_in, lax.axis_size(net_axis), axi...]
    reshape x0 -> x2, local copies, waits for them, and re-layouts: none -> 9.07 us  [see_teams(): jnp.concatenate(lax.all_to_all(jnp.stack(jnp.split(field_in, lax.axis_siz...]
    all_to_all x2 -> x0, local copies, waits for them, and re-layouts: 9.07 us -> none  [per_device(): lax.all_to_all(grouped, ('row', 'col'), split_axis=1, concat_axis=4, tile...]
    transpose x0 -> x2, local copies, waits for them, and re-layouts: none -> 8.81 us  [per_device(): jnp.transpose(grouped, (0, 3, 1, 2, 4, 5))]
    reshape x2, local copies, waits for them, and re-layouts: 15.6 us -> 9.38 us  [per_device(): jnp.transpose(grouped, (0, 3, 1, 2, 4, 5))]
  transfers between devices with their start and end apart: 4 -> 4, of which waited for: 3 -> 3; matrix products, arithmetic and copies ran while one was open for 26% -> 29% of each run, Pallas kernels for 0% -> 0%
where the time goes in v1:
time: 622 us; the launch traced here: 620 us
  waiting for transfers between devices  353 us (57%)
  local copies, waits for them, and re-layouts  139 us (22%)
  matrix products  65.7 us (11%)
  other arithmetic  38 us (6%)
  between operations  13.5 us (2%)
  starting transfers between devices  11.6 us (2%)
    all_to_all x2, waiting for transfers between devices, see_teams(): lax.all_to_all(jnp.stack(jnp.split(field_in, lax.axis_size(net_axis), axi...  268 us
    reduce_scatter x2, waiting for transfers between devices, per_device(): lax.psum_scatter(flat, 'col', scatter_dimension=2, tiled=True)  84.8 us
    dot_general x2, matrix products, per_device(): jnp.einsum('iap,pq->iaq', blocks, masked_ints, precision=lax.Precision.HI...  65.7 us
    unnamed x70, local copies, waits for them, and re-layouts  47 us
    reshape x1, local copies, waits for them, and re-layouts, per_device(): jnp.where(int_sym == 0, cycle_integrals, 0.0)  39.8 us
    select_n x1, other arithmetic, per_device(): jnp.where(int_sym == 0, cycle_integrals, 0.0)  23.1 us
    reshape x2, local copies, waits for them, and re-layouts, per_device(): masked_amps.reshape(rows, col_count, k_local, row_count, a_local, c_local)  19.8 us
  transfers between devices with their start and end apart: 4, of which 3 were waited for; matrix products, arithmetic and copies ran while one was open for 29% of the time, Pallas kernels for 0%

profile of v1, /device:TPU:0, one launch (start us, length us, event | category | flops | bytes accessed | tf_op | source)
XLA Modules:
  0.0 620.3 jit_solution(3226192076454397473)
XLA Ops:
  6.5 0.8 fusion.65
  7.3 0.8 dynamic_slice.6
  8.1 0.8 broadcast_xor_fusion
  9.6 11.0 %slice_select_fusion.1 = (f32[4,64,512,16]{2,3,1,0:T(8,128)}, f32[4,64,512,16]{2,3,1,0:T(8,128)}) fusion(f32[8,64,512,16]{2,3,1,0:T(8,128)} %param.4, s32[512,16]{0,1:T(8,128)S(1)} %broadcast_xor_fusion, s32[4,64]{1,0:T(4,128)S(1)} %get-tuple-element.7, s32[4,64]{1,0:T(4,128)S(1)} %get-tuple-element.8), kind=kLoop, calls=%fused_computation.4 | loop fusion | flops 12582912 | bytes 33589248 | tf_op jit(solution)/shard_map/jit(_where)/select_n | solution.py:86
  20.6 9.9 %reshape.183 = f32[4,8,8,4,128,16]{4,3,5,2,1,0:T(4,128)} reshape(f32[4,64,512,16]{2,3,1,0:T(8,128)} %get-tuple-element.5) | data formatting | bytes 16777216 | tf_op jit(solution)/shard_map/reshape | solution.py:87
  30.5 4.7 copy.201
  35.2 1.1 copy-done
  36.3 4.4 copy.133
  41.4 0.7 fusion.63
  50.1 0.7 fusion.51
  52.3 0.7 fusion.48
  53.0 0.7 fusion.47
  53.8 0.7 fusion.46
  63.2 1.7 fusion.33
  64.9 7.4 %all-to-all-start = ((f32[32,4,1,8,128,16]{4,5,3,1,2,0:T(8,128)}), f32[32,4,1,8,128,16]{4,5,3,1,2,0:T(8,128)}, u32[]{:S(2)}, u32[]{:S(2)}) async-start(f32[32,4,1,8,128,16]{4,5,3,1,2,0:T(8,128)} %fusion.33), calls=%async_computation | async-start | bytes 16777216 | tf_op jit(solution)/shard_map/all_to_all | solution.py:10
  72.3 9.9 %reshape.188 = f32[4,8,8,4,128,16]{4,3,5,2,1,0:T(4,128)} reshape(f32[4,64,512,16]{2,3,1,0:T(8,128)} %get-tuple-element.6) | data formatting | bytes 16777216 | tf_op jit(solution)/shard_map/reshape | solution.py:87
  82.2 4.7 copy.233
  86.9 1.1 copy-done.1
  88.0 4.4 copy.167
  113.3 0.7 fusion.3
  114.8 1.7 fusion.1
  116.4 145.4 %all-to-all-done = f32[32,4,1,8,128,16]{4,5,3,1,2,0:T(8,128)} async-done(((f32[32,4,1,8,128,16]{4,5,3,1,2,0:T(8,128)}), f32[32,4,1,8,128,16]{4,5,3,1,2,0:T(8,128)}, u32[]{:S(2)}, u32[]{:S(2)}) %all-to-all-start) | async-done | bytes 8388640 | tf_op jit(solution)/shard_map/all_to_all | solution.py:10
  261.9 3.7 all-to-all-start.1
  266.0 23.1 %fusion = f32[8,512,4,512]{3,2,1,0:T(4,128)} fusion(f32[8,512,4,512]{3,2,1,0:T(4,128)} %param.5, s32[4,512]{1,0:T(4,128)S(1)} %broadcast_xor_fusion.2, s32[8,512]{1,0:T(8,128)S(1)} %broadcast_xor_fusion.1), kind=kLoop, calls=%fused_computation.1 | loop fusion | flops 25165824 | bytes 67133440 | tf_op jit(solution)/shard_map/jit(_where)/select_n | solution.py:73
  289.1 39.8 %reshape.192 = f32[4096,2048,1]{1,0,2:T(8,128)} reshape(f32[8,512,4,512]{3,2,1,0:T(4,128)} %fusion) | data formatting | bytes 67108864 | tf_op jit(solution)/shard_map/reshape | solution.py:73
  328.9 4.5 copy.165
  333.5 32.6 %fusion.66 = f32[4,128,2048]{2,1,0:T(8,128)} fusion(f32[4,128,4096]{1,2,0:T(8,128)S(1)} %bitcast.415, f32[4096,2048,1]{1,0,2:T(8,128)} %reshape.192), kind=kOutput, calls=%fused_computation.141 | convolution fusion | flops 25769803776 | bytes 46137344 | tf_op jit(solution)/shard_map/iap,pq->iaq/dot_general | solution.py:98
  366.4 122.4 %all-to-all-done.1 = f32[32,4,1,8,128,16]{4,5,3,1,2,0:T(8,128)} async-done(((f32[32,4,1,8,128,16]{4,5,3,1,2,0:T(8,128)}), f32[32,4,1,8,128,16]{4,5,3,1,2,0:T(8,128)}, u32[]{:S(2)}, u32[]{:S(2)}) %all-to-all-start.1) | async-done | bytes 8388640 | tf_op jit(solution)/shard_map/all_to_all | solution.py:10
  488.8 4.5 copy.199
  493.3 33.0 %fusion.67 = f32[4,128,2048]{2,1,0:T(8,128)} fusion(f32[4,128,4096]{1,2,0:T(8,128)S(1)} %bitcast.414, f32[4096,2048,1]{1,0,2:T(8,128)} %reshape.192), kind=kOutput, calls=%fused_computation.142 | convolution fusion | flops 25769803776 | bytes 46137344 | tf_op jit(solution)/shard_map/iap,pq->iaq/dot_general | solution.py:98
  526.4 84.8 %reduce-scatter.5.cloned.1.call-done = f32[4,128,256]{2,1,0:T(8,128)} async-done(((f32[4,128,2048]{2,1,0:T(8,128)}), f32[4,128,256]{2,1,0:T(8,128)}) %reduce-scatter.5.cloned.1.call-update) | async-done | bytes 524304 | tf_op jit(solution)/shard_map/reduce_scatter | solution.py:106
  611.2 2.2 pad_maximum_fusion
  (71 shorter events, 41.9 us)
Async XLA Ops:
  30.5 5.8 copy-start
  64.9 197.0 %all-to-all-start = ((f32[32,4,1,8,128,16]{4,5,3,1,2,0:T(8,128)}), f32[32,4,1,8,128,16]{4,5,3,1,2,0:T(8,128)}, u32[]{:S(2)}, u32[]{:S(2)}) async-start(f32[32,4,1,8,128,16]{4,5,3,1,2,0:T(8,128)} %fusion.33), calls=%async_computation | async-start | bytes 16777216 | tf_op jit(solution)/shard_map/all_to_all | solution.py:10
  82.2 5.8 copy-start.1
  116.4 149.4 %copy-start.3 = (s32[64]{0:T(128)S(1)}, s32[64]{0:T(128)}, u32[]{:S(2)}) copy-start(s32[64]{0:T(128)} %param.6) | copy-start | bytes 772
  116.4 149.4 %copy-start.2 = (s32[512]{0:T(512)S(1)}, s32[512]{0:T(512)}, u32[]{:S(2)}) copy-start(s32[512]{0:T(512)} %param.7) | copy-start | bytes 6148
  261.9 226.9 %all-to-all-start.1 = ((f32[32,4,1,8,128,16]{4,5,3,1,2,0:T(8,128)}), f32[32,4,1,8,128,16]{4,5,3,1,2,0:T(8,128)}, u32[]{:S(2)}, u32[]{:S(2)}) async-start(f32[32,4,1,8,128,16]{4,5,3,1,2,0:T(8,128)} %fusion.1), calls=%async_computation.2 | async-start | bytes 16777216 | tf_op jit(solution)/shard_map/all_to_all | solution.py:10
  265.6 260.8 %reduce-scatter.3.cloned.1.call-start = ((), (), s32[]{:S(2)}) async-start(), calls=%async_computation.4 | async-start | bytes 4718592 | tf_op jit(solution)/shard_map/reduce_scatter | solution.py:106
  366.1 245.1 %reduce-scatter.5.cloned.1.call-start = ((), (), s32[]{:S(2)}) async-start(), calls=%async_computation.5 | async-start | bytes 4718592 | tf_op jit(solution)/shard_map/reduce_scatter | solution.py:106
Sparse Core Ops, SparseCore 0:
  366.2 149.8 reduce-scatter.2
  526.5 84.6 reduce-scatter.4
